TPU v7x, 512 devices: a whole 4x8x8 slice. The times are simulated.
512 devices in a mesh: ind: 64 (over y, z), snp: 8 (over x, core).
Axes of the slice: x: 4, y: 8, z: 8, core: 2. Of those that a mesh axis runs over, the one named last changes fastest.
Arguments:
- genotypes: int32 [4096, 16384], P('ind', 'snp'), may hold values from 0 to 2
- observed: int32 [4096, 16384], P('ind', 'snp'), may hold values from 0 to 1
- ancestry: float32 [4096, 32], P('ind'), may hold values from 0.018 to 54.6, as said below
- freqs: float32 [16384, 32], P(('snp', 'ind')), may hold values from 0.05 to 0.95
Outputs:
- ancestry_out: float32 [4096, 32], P('ind')
- freqs_out: float32 [16384, 32], P(('snp', 'ind'))
Inputs may be any that keep to these rules, and one draw needn't show every extreme that they name: `ancestry`: positive weights.
All inputs are finite; a program needn't handle non-finite values.
Results may differ from a plain program's by a relative error of at most 0.0003.
Values sent between devices are 32-bit elements; how exact they have to be, the bound alone decides.
No kernel may reach another device: no remote copies, remote signals or barrier semaphores. Data moves between devices by JAX's collectives and lax.ppermute only.
A program may use at most 64 MiB of HBM per device.

v0:
```python
import jax
import jax.numpy as jnp
from jax import lax
from jax.sharding import PartitionSpec as P

STEPS = 3
clip_low = 1e-05
high = lax.Precision.HIGHEST


def over_rows(left, right):
    return lax.dot_general(
        left, right, (((0,), (0,)), ((), ())), precision=high, preferred_element_type=jnp.float32
    )


def per_device(genotypes, observed, ancestry, freqs):
    ind_count = lax.axis_size("ind")
    snp_count = lax.axis_size("snp")
    geno = genotypes.astype(jnp.float32)
    seen = observed.astype(jnp.float32)
    hits = seen * geno
    misses = seen * (2.0 - geno)
    own_rows = freqs.shape[0]
    q_zero = ancestry / jnp.sum(ancestry, axis=1, keepdims=True)
    f_zero = lax.all_gather(freqs, "ind", axis=0, tiled=True)
    f_weight = 1.0 / ind_count
    q_weight = 1.0 / snp_count

    def em_map(q_rows, f_state):
        prob = jnp.dot(q_rows, f_state.T, precision=high, preferred_element_type=jnp.float32)
        ratio_a = hits / prob
        ratio_b = misses / (1.0 - prob)
        sum_a = jnp.dot(ratio_a, f_state, precision=high, preferred_element_type=jnp.float32)
        sum_b = jnp.dot(ratio_b, 1.0 - f_state, precision=high, preferred_element_type=jnp.float32)
        c_part = over_rows(ratio_a, q_rows)
        d_part = over_rows(ratio_b, q_rows)
        sum_a, sum_b = lax.psum((sum_a, sum_b), "snp")
        q_next = q_rows * (sum_a + sum_b)
        q_next = q_next / jnp.sum(q_next, axis=1, keepdims=True)
        c_total, d_total = lax.psum((c_part, d_part), "ind")
        f_next = f_state * c_total / (f_state * c_total + (1.0 - f_state) * d_total)
        return (q_next, f_next)

    for step in range(STEPS):
        q_one, f_one = em_map(q_zero, f_zero)
        rq = q_one - q_zero
        rf = f_one - f_zero
        first_local = q_weight * jnp.sum(rq * rq) + f_weight * jnp.sum(rf * rf)
        q_two, f_two = em_map(q_one, f_one)
        vq = q_two - 2.0 * q_one + q_zero
        vf = f_two - 2.0 * f_one + f_zero
        second_local = q_weight * jnp.sum(vq * vq) + f_weight * jnp.sum(vf * vf)
        first, second = lax.psum((first_local, second_local), ("ind", "snp"))
        alpha = -jnp.sqrt(first / (second + 1e-20))
        q_ext = jnp.clip(q_zero - 2.0 * alpha * rq + alpha * alpha * vq, clip_low, 1.0 - clip_low)
        q_zero = q_ext / jnp.sum(q_ext, axis=1, keepdims=True)
        f_zero = jnp.clip(f_zero - 2.0 * alpha * rf + alpha * alpha * vf, clip_low, 1.0 - clip_low)
    f_final = lax.dynamic_slice_in_dim(f_zero, lax.axis_index("ind") * own_rows, own_rows, 0)
    return (q_zero, f_final)


def solution(mesh):
    in_specs = (P("ind", "snp"), P("ind", "snp"), P("ind", None), P(("snp", "ind"), None))
    out_specs = (P("ind", None), P(("snp", "ind"), None))
    return jax.shard_map(
        per_device, mesh=mesh, in_specs=in_specs, out_specs=out_specs, check_vma=False
    )
```

profile of v0, /device:TPU:1, one launch (start us, length us, event | category | flops | bytes accessed | tf_op | source)
XLA Modules:
  0.0 1308.1 jit_solution(10451656634871468365)
XLA Ops:
  7.2 47.0 %all_gather.3 = f32[2048,32]{1,0:T(8,128)S(1)} all-gather(f32[32,32]{1,0:T(8,128)} %param.7), channel_id=1, replica_groups=mesh['ind'=64,'snp'=8] {'ind'}, dimensions={0}, use_global_device_ids=true | all-gather | bytes 266240 | tf_op jit(solution)/shard_map/all_gather | solution.py:26
  54.3 1.3 fusion.48
  59.1 1.8 convolution_add_fusion
  60.9 32.1 %psum.240 = f32[64,32]{0,1:T(8,128)S(1)} all-reduce(f32[64,32]{0,1:T(8,128)S(1)} %convolution_add_fusion), channel_id=1, replica_groups=mesh['ind'=64,'snp'=8] {'snp'}, use_global_device_ids=true, to_apply=%region_1.0 | all-reduce | flops 2048 | bytes 16384 | tf_op jit(solution)/shard_map/psum | solution.py:38
  93.0 123.9 %all-reduce.26.cloned.1.call-done = (f32[2048,32]{0,1:T(8,128)}, f32[2048,32]{0,1:T(8,128)}) async-done(((f32[2048,32]{0,1:T(8,128)}, f32[2048,32]{0,1:T(8,128)}), (f32[2048,32]{0,1:T(8,128)}, f32[2048,32]{0,1:T(8,128)})) %all-reduce.26.cloned.1.call-update) | async-done | bytes 524304 | tf_op jit(solution)/shard_map/psum | solution.py:41
  216.9 1.7 multiply_reduce_fusion.5
  222.9 24.9 %psum.241 = f32[64,32]{0,1:T(8,128)S(1)} all-reduce(f32[64,32]{0,1:T(8,128)S(1)} %convolution_add_fusion.5), channel_id=1, replica_groups=mesh['ind'=64,'snp'=8] {'snp'}, use_global_device_ids=true, to_apply=%region_9.0 | all-reduce | flops 2048 | bytes 16384 | tf_op jit(solution)/shard_map/psum | solution.py:38
  250.5 123.8 %all-reduce.24.cloned.1.call-done = (f32[2048,32]{0,1:T(8,128)}, f32[2048,32]{0,1:T(8,128)}) async-done(((f32[2048,32]{0,1:T(8,128)}, f32[2048,32]{0,1:T(8,128)}), (f32[2048,32]{0,1:T(8,128)}, f32[2048,32]{0,1:T(8,128)})) %all-reduce.24.cloned.1.call-update) | async-done | bytes 524304 | tf_op jit(solution)/shard_map/psum | solution.py:41
  374.3 1.7 multiply_reduce_fusion.4
  376.7 99.3 %all-reduce.2 = (f32[]{:T(128)}, f32[]{:T(128)}) all-reduce(f32[]{:T(128)S(6)} %add.164, f32[]{:T(128)S(6)} %add.169), channel_id=1, replica_groups=mesh['ind'=64,'snp'=8] {'ind','snp'}, use_global_device_ids=true, to_apply=%region_8.0 | all-reduce | flops 2 | bytes 16 | tf_op jit(solution)/shard_map/psum | solution.py:54
  481.8 20.9 %psum.242 = f32[64,32]{0,1:T(8,128)S(1)} all-reduce(f32[64,32]{0,1:T(8,128)S(1)} %convolution_add_fusion.4), channel_id=1, replica_groups=mesh['ind'=64,'snp'=8] {'snp'}, use_global_device_ids=true, to_apply=%region_18.19 | all-reduce | flops 2048 | bytes 16384 | tf_op jit(solution)/shard_map/psum | solution.py:38
  502.7 125.4 %all-reduce.22.cloned.1.call-done = (f32[2048,32]{0,1:T(8,128)}, f32[2048,32]{0,1:T(8,128)}) async-done(((f32[2048,32]{0,1:T(8,128)}, f32[2048,32]{0,1:T(8,128)}), (f32[2048,32]{0,1:T(8,128)}, f32[2048,32]{0,1:T(8,128)})) %all-reduce.22.cloned.1.call-update) | async-done | bytes 524304 | tf_op jit(solution)/shard_map/psum | solution.py:41
  628.1 1.7 multiply_reduce_fusion.3
  634.8 24.9 %psum.243 = f32[64,32]{0,1:T(8,128)S(1)} all-reduce(f32[64,32]{0,1:T(8,128)S(1)} %convolution_add_fusion.3), channel_id=1, replica_groups=mesh['ind'=64,'snp'=8] {'snp'}, use_global_device_ids=true, to_apply=%region_26.27 | all-reduce | flops 2048 | bytes 16384 | tf_op jit(solution)/shard_map/psum | solution.py:38
  661.6 123.9 %all-reduce.20.cloned.1.call-done = (f32[2048,32]{0,1:T(8,128)}, f32[2048,32]{0,1:T(8,128)}) async-done(((f32[2048,32]{0,1:T(8,128)}, f32[2048,32]{0,1:T(8,128)}), (f32[2048,32]{0,1:T(8,128)}, f32[2048,32]{0,1:T(8,128)})) %all-reduce.20.cloned.1.call-update) | async-done | bytes 524304 | tf_op jit(solution)/shard_map/psum | solution.py:41
  785.6 1.7 multiply_reduce_fusion.2
  787.9 99.4 %all-reduce.1 = (f32[]{:T(128)}, f32[]{:T(128)}) all-reduce(f32[]{:T(128)S(6)} %add.175, f32[]{:T(128)S(6)} %add.180), channel_id=1, replica_groups=mesh['ind'=64,'snp'=8] {'ind','snp'}, use_global_device_ids=true, to_apply=%region_25.26 | all-reduce | flops 2 | bytes 16 | tf_op jit(solution)/shard_map/psum | solution.py:54
  893.1 20.8 %psum.244 = f32[64,32]{0,1:T(8,128)S(1)} all-reduce(f32[64,32]{0,1:T(8,128)S(1)} %convolution_add_fusion.2), channel_id=1, replica_groups=mesh['ind'=64,'snp'=8] {'snp'}, use_global_device_ids=true, to_apply=%region_35.36 | all-reduce | flops 2048 | bytes 16384 | tf_op jit(solution)/shard_map/psum | solution.py:38
  913.9 125.4 %all-reduce.18.cloned.1.call-done = (f32[2048,32]{0,1:T(8,128)}, f32[2048,32]{0,1:T(8,128)}) async-done(((f32[2048,32]{0,1:T(8,128)}, f32[2048,32]{0,1:T(8,128)}), (f32[2048,32]{0,1:T(8,128)}, f32[2048,32]{0,1:T(8,128)})) %all-reduce.18.cloned.1.call-update) | async-done | bytes 524304 | tf_op jit(solution)/shard_map/psum | solution.py:41
  1039.3 1.7 multiply_reduce_fusion.1
  1045.9 24.9 %psum.245 = f32[64,32]{0,1:T(8,128)S(1)} all-reduce(f32[64,32]{0,1:T(8,128)S(1)} %convolution_add_fusion.1), channel_id=1, replica_groups=mesh['ind'=64,'snp'=8] {'snp'}, use_global_device_ids=true, to_apply=%region_43.44 | all-reduce | flops 2048 | bytes 16384 | tf_op jit(solution)/shard_map/psum | solution.py:38
  1072.8 124.0 %all-reduce.16.cloned.1.call-done = (f32[2048,32]{0,1:T(8,128)}, f32[2048,32]{0,1:T(8,128)}) async-done(((f32[2048,32]{0,1:T(8,128)}, f32[2048,32]{0,1:T(8,128)}), (f32[2048,32]{0,1:T(8,128)}, f32[2048,32]{0,1:T(8,128)})) %all-reduce.16.cloned.1.call-update) | async-done | bytes 524304 | tf_op jit(solution)/shard_map/psum | solution.py:41
  1196.8 1.7 multiply_reduce_fusion
  1199.2 99.3 %all-reduce = (f32[]{:T(128)}, f32[]{:T(128)}) all-reduce(f32[]{:T(128)S(6)} %add.186, f32[]{:T(128)S(6)} %add.191), channel_id=1, replica_groups=mesh['ind'=64,'snp'=8] {'ind','snp'}, use_global_device_ids=true, to_apply=%region_42.43 | all-reduce | flops 2 | bytes 16 | tf_op jit(solution)/shard_map/psum | solution.py:54
  (66 shorter events, 28.6 us)
Async XLA Ops:
  7.2 47.0 %copy-start.2 = (f32[64,32]{0,1:T(8,128)S(1)}, f32[64,32]{0,1:T(8,128)}, u32[]{:S(2)}) copy-start(f32[64,32]{0,1:T(8,128)} %param.6) | copy-start | bytes 24580
  7.2 209.7 %all-reduce.26.cloned.1.call-start = ((), (), s32[]{:S(2)}) async-start(), calls=%async_computation.5 | async-start | bytes 1048576 | tf_op jit(solution)/shard_map/psum | solution.py:41
  54.2 1.3 copy-start
  54.2 1.3 copy-start.1
  58.2 316.1 %all-reduce.24.cloned.1.call-start = ((), (), s32[]{:S(2)}) async-start(), calls=%async_computation.4 | async-start | bytes 1048576 | tf_op jit(solution)/shard_map/psum | solution.py:41
  221.7 406.4 %all-reduce.22.cloned.1.call-start = ((), (), s32[]{:S(2)}) async-start(), calls=%async_computation.3 | async-start | bytes 1048576 | tf_op jit(solution)/shard_map/psum | solution.py:41
  480.6 305.0 %all-reduce.20.cloned.1.call-start = ((), (), s32[]{:S(2)}) async-start(), calls=%async_computation.2 | async-start | bytes 1048576 | tf_op jit(solution)/shard_map/psum | solution.py:41
  632.9 406.4 %all-reduce.18.cloned.1.call-start = ((), (), s32[]{:S(2)}) async-start(), calls=%async_computation.1 | async-start | bytes 1048576 | tf_op jit(solution)/shard_map/psum | solution.py:41
  891.8 304.9 %all-reduce.16.cloned.1.call-start = ((), (), s32[]{:S(2)}) async-start(), calls=%async_computation | async-start | bytes 1048576 | tf_op jit(solution)/shard_map/psum | solution.py:41
Sparse Core Ops, SparseCore 0:
  58.3 158.5 all-reduce.25
  221.8 152.4 all-reduce.23
  480.7 147.3 all-reduce.21
  633.0 152.4 all-reduce.19
  892.0 147.2 all-reduce.17
  1044.2 152.5 all-reduce.15
where the time goes:
time: 1310 us
  waiting for transfers between devices  746 us (57%)
  blocking collectives  494 us (38%)
  matrix products  27.2 us (2%)
  between operations  26.2 us (2%)
  other arithmetic  13.5 us (1%)
    psum x6, waiting for transfers between devices, em_map(): c_total, d_total = lax.psum((c_part, d_part), 'ind')  746 us
    psum x3, blocking collectives, per_device(): first, second = lax.psum((first_local, second_local), ('ind', 'snp'))  298 us
    psum x6, blocking collectives, em_map(): sum_a, sum_b = lax.psum((sum_a, sum_b), 'snp')  148 us
    all_gather x1, blocking collectives, per_device(): f_zero = lax.all_gather(freqs, 'ind', axis=0, tiled=True)  47 us
  transfers between devices with their start and end apart: 6, of which 6 were waited for; matrix products, arithmetic and copies ran while one was open for 1% of the time, Pallas kernels for 0%

commit v1 on v0

--- a/solution.py
+++ b/solution.py
@@ -6,6 +6,11 @@
 STEPS = 3
 clip_low = 1e-05
 high = lax.Precision.HIGHEST
+
+
+def axis_by_axis(x, inner_axis, outer_axis):
+    inner = lax.psum(x, inner_axis)
+    return lax.psum(inner, outer_axis)
 
 
 def over_rows(left, right):
@@ -51,7 +56,7 @@
         vq = q_two - 2.0 * q_one + q_zero
         vf = f_two - 2.0 * f_one + f_zero
         second_local = q_weight * jnp.sum(vq * vq) + f_weight * jnp.sum(vf * vf)
-        first, second = lax.psum((first_local, second_local), ("ind", "snp"))
+        first, second = axis_by_axis((first_local, second_local), "ind", "snp")
         alpha = -jnp.sqrt(first / (second + 1e-20))
         q_ext = jnp.clip(q_zero - 2.0 * alpha * rq + alpha * alpha * vq, clip_low, 1.0 - clip_low)
         q_zero = q_ext / jnp.sum(q_ext, axis=1, keepdims=True)

time: 1310 us -> 1480 us (1.13)
  blocking collectives: 494 us -> 673 us
    psum x3 -> x6, blocking collectives: 298 us -> 477 us  [the longest x3 341 us: axis_by_axis(): inner = lax.psum(x, inner_axis)]
where the time goes in v1:
time: 1480 us
  waiting for transfers between devices  739 us (50%)
  blocking collectives  673 us (45%)
  matrix products  27.2 us (2%)
  between operations  26.2 us (2%)
    psum x6, waiting for transfers between devices, em_map(): c_total, d_total = lax.psum((c_part, d_part), 'ind')  739 us
    psum x3, blocking collectives, axis_by_axis(): inner = lax.psum(x, inner_axis)  341 us
    psum x6, blocking collectives, em_map(): sum_a, sum_b = lax.psum((sum_a, sum_b), 'snp')  149 us
    psum x3, blocking collectives, axis_by_axis(): return lax.psum(inner, outer_axis)  136 us
    all_gather x1, blocking collectives, per_device(): f_zero = lax.all_gather(freqs, 'ind', axis=0, tiled=True)  47 us
  transfers between devices with their start and end apart: 6, of which 6 were waited for; matrix products, arithmetic and copies ran while one was open for 1% of the time, Pallas kernels for 0%

profile of v1, /device:TPU:1, one launch (start us, length us, event | category | flops | bytes accessed | tf_op | source)
XLA Modules:
  0.0 1479.9 jit_solution(11154453667311599493)
XLA Ops:
  7.2 47.0 %all_gather.3 = f32[2048,32]{1,0:T(8,128)S(1)} all-gather(f32[32,32]{1,0:T(8,128)} %param.7), channel_id=1, replica_groups=mesh['ind'=64,'snp'=8] {'ind'}, dimensions={0}, use_global_device_ids=true | all-gather | bytes 266240 | tf_op jit(solution)/shard_map/all_gather | solution.py:31
  59.1 1.8 convolution_add_fusion
  60.9 32.1 %psum.288 = f32[64,32]{0,1:T(8,128)S(1)} all-reduce(f32[64,32]{0,1:T(8,128)S(1)} %convolution_add_fusion), channel_id=1, replica_groups=mesh['ind'=64,'snp'=8] {'snp'}, use_global_device_ids=true, to_apply=%region_1.0 | all-reduce | flops 2048 | bytes 16384 | tf_op jit(solution)/shard_map/psum | solution.py:43
  93.0 123.9 %all-reduce.29.cloned.1.call-done = (f32[2048,32]{0,1:T(8,128)}, f32[2048,32]{0,1:T(8,128)}) async-done(((f32[2048,32]{0,1:T(8,128)}, f32[2048,32]{0,1:T(8,128)}), (f32[2048,32]{0,1:T(8,128)}, f32[2048,32]{0,1:T(8,128)})) %all-reduce.29.cloned.1.call-update) | async-done | bytes 524304 | tf_op jit(solution)/shard_map/psum | solution.py:46
  222.9 24.9 %psum.289 = f32[64,32]{0,1:T(8,128)S(1)} all-reduce(f32[64,32]{0,1:T(8,128)S(1)} %convolution_add_fusion.5), channel_id=1, replica_groups=mesh['ind'=64,'snp'=8] {'snp'}, use_global_device_ids=true, to_apply=%region_10.0 | all-reduce | flops 2048 | bytes 16384 | tf_op jit(solution)/shard_map/psum | solution.py:43
  250.5 123.8 %all-reduce.27.cloned.1.call-done = (f32[2048,32]{0,1:T(8,128)}, f32[2048,32]{0,1:T(8,128)}) async-done(((f32[2048,32]{0,1:T(8,128)}, f32[2048,32]{0,1:T(8,128)}), (f32[2048,32]{0,1:T(8,128)}, f32[2048,32]{0,1:T(8,128)})) %all-reduce.27.cloned.1.call-update) | async-done | bytes 524304 | tf_op jit(solution)/shard_map/psum | solution.py:46
  374.3 1.7 multiply_reduce_fusion.4
  376.7 113.6 %all-reduce.2 = (f32[]{:T(128)}, f32[]{:T(128)}) all-reduce(f32[]{:T(128)S(6)} %add.176, f32[]{:T(128)S(6)} %add.181), channel_id=1, replica_groups=mesh['ind'=64,'snp'=8] {'ind'}, use_global_device_ids=true, to_apply=%region_8.0 | all-reduce | flops 2 | bytes 16 | tf_op jit(solution)/shard_map/psum | solution.py:12
  490.3 45.3 %all-reduce.11 = (f32[]{:T(128)}, f32[]{:T(128)}) all-reduce(f32[]{:T(128)} %get-tuple-element.16, f32[]{:T(128)} %get-tuple-element.17), channel_id=1, replica_groups=mesh['ind'=64,'snp'=8] {'snp'}, use_global_device_ids=true, to_apply=%region_9.0 | all-reduce | flops 2 | bytes 16 | tf_op jit(solution)/shard_map/psum | solution.py:13
  541.3 21.2 %psum.290 = f32[64,32]{0,1:T(8,128)S(1)} all-reduce(f32[64,32]{0,1:T(8,128)S(1)} %convolution_add_fusion.4), channel_id=1, replica_groups=mesh['ind'=64,'snp'=8] {'snp'}, use_global_device_ids=true, to_apply=%region_20.21 | all-reduce | flops 2048 | bytes 16384 | tf_op jit(solution)/shard_map/psum | solution.py:43
  562.6 121.6 %all-reduce.25.cloned.1.call-done = (f32[2048,32]{0,1:T(8,128)}, f32[2048,32]{0,1:T(8,128)}) async-done(((f32[2048,32]{0,1:T(8,128)}, f32[2048,32]{0,1:T(8,128)}), (f32[2048,32]{0,1:T(8,128)}, f32[2048,32]{0,1:T(8,128)})) %all-reduce.25.cloned.1.call-update) | async-done | bytes 524304 | tf_op jit(solution)/shard_map/psum | solution.py:46
  684.2 1.7 multiply_reduce_fusion.3
  690.9 24.9 %psum.291 = f32[64,32]{0,1:T(8,128)S(1)} all-reduce(f32[64,32]{0,1:T(8,128)S(1)} %convolution_add_fusion.3), channel_id=1, replica_groups=mesh['ind'=64,'snp'=8] {'snp'}, use_global_device_ids=true, to_apply=%region_29.30 | all-reduce | flops 2048 | bytes 16384 | tf_op jit(solution)/shard_map/psum | solution.py:43
  717.7 123.9 %all-reduce.23.cloned.1.call-done = (f32[2048,32]{0,1:T(8,128)}, f32[2048,32]{0,1:T(8,128)}) async-done(((f32[2048,32]{0,1:T(8,128)}, f32[2048,32]{0,1:T(8,128)}), (f32[2048,32]{0,1:T(8,128)}, f32[2048,32]{0,1:T(8,128)})) %all-reduce.23.cloned.1.call-update) | async-done | bytes 524304 | tf_op jit(solution)/shard_map/psum | solution.py:46
  841.7 1.7 multiply_reduce_fusion.2
  844.1 113.6 %all-reduce.1 = (f32[]{:T(128)}, f32[]{:T(128)}) all-reduce(f32[]{:T(128)S(6)} %add.187, f32[]{:T(128)S(6)} %add.192), channel_id=1, replica_groups=mesh['ind'=64,'snp'=8] {'ind'}, use_global_device_ids=true, to_apply=%region_27.28 | all-reduce | flops 2 | bytes 16 | tf_op jit(solution)/shard_map/psum | solution.py:12
  957.6 45.3 %all-reduce.10 = (f32[]{:T(128)}, f32[]{:T(128)}) all-reduce(f32[]{:T(128)} %get-tuple-element.14, f32[]{:T(128)} %get-tuple-element.15), channel_id=1, replica_groups=mesh['ind'=64,'snp'=8] {'snp'}, use_global_device_ids=true, to_apply=%region_28.29 | all-reduce | flops 2 | bytes 16 | tf_op jit(solution)/shard_map/psum | solution.py:13
  1008.7 20.9 %psum.292 = f32[64,32]{0,1:T(8,128)S(1)} all-reduce(f32[64,32]{0,1:T(8,128)S(1)} %convolution_add_fusion.2), channel_id=1, replica_groups=mesh['ind'=64,'snp'=8] {'snp'}, use_global_device_ids=true, to_apply=%region_39.40 | all-reduce | flops 2048 | bytes 16384 | tf_op jit(solution)/shard_map/psum | solution.py:43
  1029.6 122.0 %all-reduce.21.cloned.1.call-done = (f32[2048,32]{0,1:T(8,128)}, f32[2048,32]{0,1:T(8,128)}) async-done(((f32[2048,32]{0,1:T(8,128)}, f32[2048,32]{0,1:T(8,128)}), (f32[2048,32]{0,1:T(8,128)}, f32[2048,32]{0,1:T(8,128)})) %all-reduce.21.cloned.1.call-update) | async-done | bytes 524304 | tf_op jit(solution)/shard_map/psum | solution.py:46
  1158.2 24.9 %psum.293 = f32[64,32]{0,1:T(8,128)S(1)} all-reduce(f32[64,32]{0,1:T(8,128)S(1)} %convolution_add_fusion.1), channel_id=1, replica_groups=mesh['ind'=64,'snp'=8] {'snp'}, use_global_device_ids=true, to_apply=%region_48.49 | all-reduce | flops 2048 | bytes 16384 | tf_op jit(solution)/shard_map/psum | solution.py:43
  1185.1 123.9 %all-reduce.19.cloned.1.call-done = (f32[2048,32]{0,1:T(8,128)}, f32[2048,32]{0,1:T(8,128)}) async-done(((f32[2048,32]{0,1:T(8,128)}, f32[2048,32]{0,1:T(8,128)}), (f32[2048,32]{0,1:T(8,128)}, f32[2048,32]{0,1:T(8,128)})) %all-reduce.19.cloned.1.call-update) | async-done | bytes 524304 | tf_op jit(solution)/shard_map/psum | solution.py:46
  1309.0 1.7 multiply_reduce_fusion
  1311.4 113.6 %all-reduce = (f32[]{:T(128)}, f32[]{:T(128)}) all-reduce(f32[]{:T(128)S(6)} %add.198, f32[]{:T(128)S(6)} %add.203), channel_id=1, replica_groups=mesh['ind'=64,'snp'=8] {'ind'}, use_global_device_ids=true, to_apply=%region_46.47 | all-reduce | flops 2 | bytes 16 | tf_op jit(solution)/shard_map/psum | solution.py:12
  1425.0 45.3 %all-reduce.9 = (f32[]{:T(128)}, f32[]{:T(128)}) all-reduce(f32[]{:T(128)} %get-tuple-element.12, f32[]{:T(128)} %get-tuple-element.13), channel_id=1, replica_groups=mesh['ind'=64,'snp'=8] {'snp'}, use_global_device_ids=true, to_apply=%region_47.48 | all-reduce | flops 2 | bytes 16 | tf_op jit(solution)/shard_map/psum | solution.py:13
  (69 shorter events, 33.3 us)
Async XLA Ops:
  7.2 47.0 %copy-start.2 = (f32[64,32]{0,1:T(8,128)S(1)}, f32[64,32]{0,1:T(8,128)}, u32[]{:S(2)}) copy-start(f32[64,32]{0,1:T(8,128)} %param.6) | copy-start | bytes 24580
  7.2 209.7 %all-reduce.29.cloned.1.call-start = ((), (), s32[]{:S(2)}) async-start(), calls=%async_computation.5 | async-start | bytes 1048576 | tf_op jit(solution)/shard_map/psum | solution.py:46
  54.2 1.3 copy-start
  54.2 1.3 copy-start.1
  58.2 316.1 %all-reduce.27.cloned.1.call-start = ((), (), s32[]{:S(2)}) async-start(), calls=%async_computation.4 | async-start | bytes 1048576 | tf_op jit(solution)/shard_map/psum | solution.py:46
  221.7 462.5 %all-reduce.25.cloned.1.call-start = ((), (), s32[]{:S(2)}) async-start(), calls=%async_computation.3 | async-start | bytes 1048576 | tf_op jit(solution)/shard_map/psum | solution.py:46
  540.1 301.6 %all-reduce.23.cloned.1.call-start = ((), (), s32[]{:S(2)}) async-start(), calls=%async_computation.2 | async-start | bytes 1048576 | tf_op jit(solution)/shard_map/psum | solution.py:46
  689.0 462.6 %all-reduce.21.cloned.1.call-start = ((), (), s32[]{:S(2)}) async-start(), calls=%async_computation.1 | async-start | bytes 1048576 | tf_op jit(solution)/shard_map/psum | solution.py:46
  1007.5 301.6 %all-reduce.19.cloned.1.call-start = ((), (), s32[]{:S(2)}) async-start(), calls=%async_computation | async-start | bytes 1048576 | tf_op jit(solution)/shard_map/psum | solution.py:46
Sparse Core Ops, SparseCore 0:
  58.3 158.5 all-reduce.28
  221.8 152.4 all-reduce.26
  540.2 143.9 all-reduce.24
  689.1 152.4 all-reduce.22
  1007.6 143.9 all-reduce.20
  1156.5 152.4 all-reduce.18
